TPU v7x, 256 devices: a whole 4x4x8 slice. The times are simulated.
256 devices in a mesh: seq: 64 (over y, z, core), head: 4 (over x).
Axes of the slice: x: 4, y: 4, z: 8, core: 2. Of those that a mesh axis runs over, the one named last changes fastest.
Arguments:
- queries: bfloat16 [8192, 1024], P('seq', 'head'), may hold values from -6 to 6
- raw_keys: bfloat16 [8192, 1024], P('seq', 'head'), may hold values from -6 to 6
- values: bfloat16 [8192, 1024], P('seq', 'head'), may hold values from -6 to 6
- write_rate: float32 [8192, 8], P('seq', 'head'), may hold values from 0.0005 to 1
- out_weight: bfloat16 [1024, 1024], P('head'), may hold values from -0.1875 to 0.1875
- out_grad: bfloat16 [8192, 1024], P('seq', 'head'), may hold values from -6 to 6
Outputs:
- layer_out: bfloat16 [8192, 1024], P('seq', 'head')
- query_grad: bfloat16 [8192, 1024], P('seq', 'head')
- key_grad: bfloat16 [8192, 1024], P('seq', 'head')
- value_grad: bfloat16 [8192, 1024], P('seq', 'head')
- rate_grad: float32 [8192, 8], P('seq', 'head')
All inputs are finite; a program needn't handle non-finite values.
Results may differ from a plain program's by a relative error of at most 0.0049.
Values may be sent and summed in bfloat16 or wider, within the bound.
No kernel may reach another device: no remote copies, remote signals or barrier semaphores. Data moves between devices by JAX's collectives and lax.ppermute only.
A program may use at most 128 MiB of HBM per device.

v0:
```python
import jax
import jax.numpy as jnp
from jax import lax
from jax.sharding import PartitionSpec as P


BLOCK = 64


epsilon = 1e-06
highest = lax.Precision.HIGHEST


def unit_rows(array):
    return array * lax.rsqrt(jnp.sum(array * array, -1, keepdims=True) + epsilon)


def to_blocks(array, head_count):
    rows = array.shape[0]
    head_width = array.shape[1] // head_count
    return array.reshape(rows // BLOCK, BLOCK, head_count, head_width)


def rate_blocks(decay_rate):
    rows = decay_rate.shape[0]
    head_count = decay_rate.shape[1]
    return decay_rate.reshape(rows // BLOCK, BLOCK, head_count)


def from_blocks(block_outputs):
    block_count, size, head_count, head_width = block_outputs.shape
    return block_outputs.reshape(block_count * size, head_count * head_width)


@jax.custom_vjp
def unit_lower_inverse(strict_lower):
    return unit_lower_inverse_fwd(strict_lower)[0]


def unit_lower_inverse_fwd(strict_lower):
    size = strict_lower.shape[-1]
    result = jnp.eye(size, dtype=jnp.float32) - strict_lower
    power_term = jnp.einsum("hnij,hnjk->hnik", strict_lower, strict_lower, precision=highest)
    span_done = 2
    while span_done < size:
        both = jnp.einsum(
            "hnij,hnjk->hnik",
            jnp.concatenate([power_term, result], -2),
            power_term,
            precision=highest,
        )
        power_term = both[..., :size, :]
        result = result + both[..., size:, :]
        span_done = span_done * 2
    return result, result


def unit_lower_inverse_bwd(result, grad):
    inner = jnp.einsum("hnji,hnjk->hnik", result, grad, precision=highest)
    outer = jnp.einsum("hnij,hnkj->hnik", inner, result, precision=highest)
    return (jnp.tril(-outer, -1),)


unit_lower_inverse.defvjp(unit_lower_inverse_fwd, unit_lower_inverse_bwd)


def block_factors(query_blocks, key_blocks, value_blocks, rate_parts):
    unit_query = unit_rows(query_blocks)
    unit_key = unit_rows(key_blocks)
    key_gram = jnp.einsum(
        "nchd,nshd->hncs", unit_key * rate_parts[..., None], unit_key, precision=highest
    )
    strict_lower = jnp.tril(key_gram, -1)
    result = unit_lower_inverse(strict_lower)
    scaled = result * jnp.transpose(rate_parts, (2, 0, 1))[..., None, :]
    key_mix = jnp.einsum("hncs,nshd->nchd", scaled, unit_key, precision=highest)
    value_mix = jnp.einsum("hncs,nshd->nchd", scaled, value_blocks, precision=highest)
    causal_scores = jnp.tril(jnp.einsum("nchd,nshd->hncs", unit_query, unit_key, precision=highest))
    return (unit_query, unit_key, key_mix, value_mix, causal_scores)


def run_blocks(factors, start_state):
    unit_query, unit_key, key_mix, value_mix, causal_scores = factors
    moved = (unit_query, unit_key, key_mix, value_mix, jnp.moveaxis(causal_scores, 1, 0))

    def advance_block(state, pieces):
        unit_query, unit_key, key_mix, value_mix, causal_scores = pieces
        innovation = value_mix - jnp.einsum("chd,hde->che", key_mix, state, precision=highest)
        block_out = jnp.einsum("chd,hde->che", unit_query, state, precision=highest)
        block_out = block_out + jnp.einsum(
            "hcs,she->che", causal_scores, innovation, precision=highest
        )
        state = state + jnp.einsum("chd,che->hde", unit_key, innovation, precision=highest)
        return (state, block_out)

    return lax.scan(advance_block, start_state, moved, unroll=True)


def mm(left, right):
    return jnp.einsum("hij,hjk->hik", left, right, precision=highest)


def mm_t(left, right):
    return jnp.einsum("hji,hjk->hik", left, right, precision=highest)


def pick_head(array, index):
    return lax.dynamic_slice_in_dim(array, index, 1, 0)


def scan_both(transition, offset, local_adjoint, count, axis):
    place = lax.axis_index(axis)
    width = transition.shape[-1]
    core = place % 2
    own = jnp.concatenate([transition, offset, local_adjoint], -1)
    got = lax.ppermute(pick_head(own, 1 - core), axis, [(i, i ^ 1) for i in range(count)])
    mine = pick_head(own, core)
    second = core == 1
    low = jnp.where(second, got, mine)
    high = jnp.where(second, mine, got)
    core_low, core_high = low, high
    joined = mm(high[..., :width], jnp.concatenate([low[..., :width], low[..., width : 2 * width]], -1))
    total_map = joined[..., :width]
    total_shift = joined[..., width:] + high[..., width : 2 * width]
    total_adjoint = mm_t(low[..., :width], high[..., 2 * width :]) + low[..., 2 * width :]
    entry_map = entry_state = exit_map = exit_adjoint = None
    step = 2
    while step < count:
        last = 2 * step >= count
        pairs = [(i, i ^ step) for i in range(count)]
        upper = (place & step) != 0
        if last:
            sent = jnp.concatenate([total_shift, total_adjoint], -1)
        else:
            sent = jnp.concatenate([total_map, total_shift, total_adjoint], -1)
        got = lax.ppermute(sent, axis, pairs)
        low = jnp.where(upper, got, sent)
        high = jnp.where(upper, sent, got)
        if last:
            low_shift = low[..., :width]
            high_adjoint = high[..., width:]
        else:
            low_map, low_shift = low[..., :width], low[..., width : 2 * width]
            high_map, high_adjoint = high[..., :width], high[..., 2 * width :]
        if entry_map is None:
            entry_state = jnp.where(upper, low_shift, jnp.zeros_like(low_shift))
            exit_adjoint = jnp.where(upper, jnp.zeros_like(high_adjoint), high_adjoint)
            if not last:
                eye = jnp.broadcast_to(jnp.eye(width, dtype=jnp.float32), low_map.shape)
                entry_map = jnp.where(upper, low_map, eye)
                exit_map = jnp.where(upper, eye, jnp.swapaxes(high_map, 1, 2))
        else:
            entry_state = jnp.where(upper, entry_state + mm(entry_map, low_shift), entry_state)
            exit_adjoint = jnp.where(upper, exit_adjoint, exit_adjoint + mm(exit_map, high_adjoint))
            if not last:
                entry_map = jnp.where(upper, mm(entry_map, low_map), entry_map)
                exit_map = jnp.where(
                    upper, exit_map, jnp.einsum("hij,hkj->hik", exit_map, high_map, precision=highest)
                )
        if not last:
            joined = mm(high_map, jnp.concatenate([low_map, low_shift], -1))
            total_map = joined[..., :width]
            total_shift = joined[..., width:] + high[..., width : 2 * width]
            total_adjoint = mm_t(low_map, high_adjoint) + low[..., 2 * width :]
        step *= 2
    if entry_state is None:
        entry_state = jnp.zeros_like(total_shift)
        exit_adjoint = jnp.zeros_like(total_adjoint)
    entry_second = mm(core_low[..., :width], entry_state) + core_low[..., width : 2 * width]
    exit_first = mm_t(core_high[..., :width], exit_adjoint) + core_high[..., 2 * width :]
    mine = jnp.concatenate(
        [jnp.where(second, entry_second, entry_state), jnp.where(second, exit_adjoint, exit_first)], -1
    )
    other = jnp.concatenate(
        [jnp.where(second, entry_state, entry_second), jnp.where(second, exit_first, exit_adjoint)], -1
    )
    back = lax.ppermute(other, axis, [(i, i ^ 1) for i in range(count)])
    both = jnp.where(second, jnp.concatenate([back, mine], 0), jnp.concatenate([mine, back], 0))
    return both[..., :width], both[..., width:]


def head_ring(part, count, axis):
    return [part] + [
        lax.ppermute(part, axis, [(i, (i + k) % count) for i in range(count)])
        for k in range(1, count)
    ]


def make_body(seq_count, head_devices):
    def body(queries, raw_keys, values, write_rate, out_weight, out_grad):
        head_count = write_rate.shape[1]
        head_width = queries.shape[1] // head_count
        token_count = queries.shape[0]
        width = queries.shape[1]
        here = lax.axis_index("head")

        grad_parts = head_ring(out_grad, head_devices, "head")

        weight_rows = jnp.concatenate(
            [
                lax.dynamic_slice_in_dim(
                    out_weight, ((here - k) % head_devices) * width, width, 1
                )
                for k in range(head_devices)
            ],
            1,
        )

        def factor_inputs(float_query, float_key, float_value, rates):
            return block_factors(
                to_blocks(float_query, head_count),
                to_blocks(float_key, head_count),
                to_blocks(float_value, head_count),
                rate_blocks(rates),
            )

        factors, pull_factors = jax.vjp(
            factor_inputs,
            queries.astype(jnp.float32),
            raw_keys.astype(jnp.float32),
            values.astype(jnp.float32),
            write_rate,
        )
        unit_query, unit_key, key_mix, value_mix, causal_scores = factors
        identity_heads = jnp.broadcast_to(
            jnp.eye(head_width, dtype=jnp.float32), (head_count, head_width, head_width)
        )
        zero_heads = jnp.zeros((head_count, head_width, head_width), jnp.float32)
        widened = (
            unit_query,
            unit_key,
            key_mix,
            jnp.concatenate([jnp.zeros_like(value_mix), value_mix], -1),
            causal_scores,
        )
        joined_state, joined_outputs = run_blocks(
            widened, jnp.concatenate([identity_heads, zero_heads], -1)
        )
        transition = joined_state[..., :head_width]
        offset = joined_state[..., head_width:]
        query_effect = joined_outputs[..., :head_width]
        attended_grad = lax.dot_general(
            jnp.concatenate(grad_parts, 1),
            weight_rows,
            (((1,), (1,)), ((), ())),
            preferred_element_type=jnp.float32,
        )
        grad_blocks = attended_grad.reshape(token_count // BLOCK, BLOCK, head_count, head_width)
        local_adjoint = jnp.einsum("nchd,nche->hde", query_effect, grad_blocks, precision=highest)
        weight_cols = [lax.dynamic_slice_in_dim(out_weight, here * width, width, 1)]
        for k in range(1, head_devices):
            block = lax.dynamic_slice_in_dim(
                out_weight, ((here + k) % head_devices) * width, width, 1
            )
            weight_cols.append(
                lax.ppermute(
                    block, "head", [(i, (i + k) % head_devices) for i in range(head_devices)]
                )
            )
        weight_mine = jnp.concatenate(weight_cols, 0)
        entry_state, exit_adjoint = scan_both(transition, offset, local_adjoint, seq_count, "seq")

        def run_from_entry(factor_tuple):
            return run_blocks(factor_tuple, entry_state)

        (final_state, block_outputs), pull_run = jax.vjp(run_from_entry, factors)
        attended_bf = from_blocks(block_outputs).astype(jnp.bfloat16)
        if head_devices == 4:
            first = lax.ppermute(attended_bf, "head", [(i, (i + 1) % 4) for i in range(4)])
            second = lax.ppermute(
                jnp.stack([attended_bf, first]), "head", [(i, (i + 2) % 4) for i in range(4)]
            )
            attended_parts = [attended_bf, first, second[0], second[1]]
        else:
            attended_parts = head_ring(attended_bf, head_devices, "head")
        layer_out = jnp.dot(
            jnp.concatenate(attended_parts, 1), weight_mine, preferred_element_type=jnp.float32
        ).astype(jnp.bfloat16)
        factor_grads = pull_run((exit_adjoint, grad_blocks))
        query_part, key_part, value_part, rate_grad = pull_factors(factor_grads[0])
        return (
            layer_out,
            query_part.astype(jnp.bfloat16),
            key_part.astype(jnp.bfloat16),
            value_part.astype(jnp.bfloat16),
            rate_grad,
        )

    return body


def solution(mesh):
    placed = (
        P("seq", "head"),
        P("seq", "head"),
        P("seq", "head"),
        P("seq", "head"),
        P("head", None),
        P("seq", "head"),
    )
    return jax.shard_map(
        make_body(mesh.shape["seq"], mesh.shape["head"]),
        mesh=mesh,
        in_specs=placed,
        out_specs=(
            P("seq", "head"),
            P("seq", "head"),
            P("seq", "head"),
            P("seq", "head"),
            P("seq", "head"),
        ),
        check_vma=False,
    )
```

profile of v0, /device:TPU:8, one launch (start us, length us, event | category | flops | bytes accessed | tf_op | source)
XLA Modules:
  0.0 97.2 jit_solution(15032909571810992929)
XLA Ops:
  0.6 3.1 %collective-permute-start.1 = (bf16[128,256]{1,0:T(8,128)(2,1)}, bf16[128,256]{1,0:T(8,128)(2,1)S(1)}, u32[]{:S(2)}, u32[]{:S(2)}) collective-permute-start(bf16[128,256]{1,0:T(8,128)(2,1)} %param.11), channel_id=1, source_target_pairs={{0,2},{1,3},{2,0},{3,1},{4,6},{5,7},{6,4},{7,5},{8,10},{9,11},{10,... | collective-permute-start | bytes 196616 | tf_op jit(solution)/shard_map/ppermute | solution.py:184
  4.3 2.6 %collective-permute-start.2 = (bf16[128,256]{1,0:T(8,128)(2,1)}, bf16[128,256]{1,0:T(8,128)(2,1)S(1)}, u32[]{:S(2)}, u32[]{:S(2)}) collective-permute-start(bf16[128,256]{1,0:T(8,128)(2,1)} %param.11), channel_id=1, source_target_pairs={{0,3},{1,0},{2,1},{3,2},{4,7},{5,4},{6,5},{7,6},{8,11},{9,8},{10,9... | collective-permute-start | bytes 196616 | tf_op jit(solution)/shard_map/ppermute | solution.py:184
  7.0 0.7 copy-done.4
  7.9 0.8 copy-done.1
  9.2 0.7 copy-done.2
  16.9 0.8 constant_dynamic-slice_fusion.7
  19.5 1.4 %collective-permute-done.3 = f32[1,128,384]{2,1,0:T(8,128)S(1)} collective-permute-done((f32[1,128,384]{2,1,0:T(8,128)S(1)}, f32[1,128,384]{2,1,0:T(8,128)S(1)}, u32[]{:S(2)}, u32[]{:S(2)}) %collective-permute-start.3) | collective-permute-done | bytes 196640 | tf_op jit(solution)/shard_map/ppermute | solution.py:116
  21.5 2.0 %collective-permute-start.4 = (f32[1,128,384]{2,1,0:T(8,128)S(1)}, f32[1,128,384]{2,1,0:T(8,128)S(1)}, u32[]{:S(2)}, u32[]{:S(2)}) collective-permute-start(f32[1,128,384]{2,1,0:T(8,128)S(1)} %pad_maximum_fusion), channel_id=1, source_target_pairs={{0,8},{4,12},{8,0},{12,4},{16,24},{20,28},{24,16},{28,20},{32,40},... | collective-permute-start | bytes 589832 | tf_op jit(solution)/shard_map/ppermute | solution.py:136
  23.5 3.2 %collective-permute-start.14 = (bf16[256,256]{1,0:T(8,128)(2,1)}, bf16[256,256]{1,0:T(8,128)(2,1)}, u32[]{:S(2)}, u32[]{:S(2)}) collective-permute-start(bf16[256,256]{1,0:T(8,128)(2,1)} %get-tuple-element.15), channel_id=1, source_target_pairs={{0,3},{1,0},{2,1},{3,2},{4,7},{5,4},{6,5},{7,6},{8,11},{9,8},{10,9... | collective-permute-start | bytes 393224 | tf_op jit(solution)/shard_map/ppermute | solution.py:256
  26.8 2.0 %collective-permute-done.4 = f32[1,128,384]{2,1,0:T(8,128)S(1)} collective-permute-done((f32[1,128,384]{2,1,0:T(8,128)S(1)}, f32[1,128,384]{2,1,0:T(8,128)S(1)}, u32[]{:S(2)}, u32[]{:S(2)}) %collective-permute-start.4) | collective-permute-done | bytes 196640 | tf_op jit(solution)/shard_map/ppermute | solution.py:136
  29.4 3.3 %collective-permute-start.5 = (f32[1,128,384]{2,1,0:T(8,128)S(1)}, f32[1,128,384]{2,1,0:T(8,128)S(1)}, u32[]{:S(2)}, u32[]{:S(2)}) collective-permute-start(f32[1,128,384]{2,1,0:T(8,128)S(1)} %pad_maximum_fusion.1), channel_id=1, source_target_pairs={{0,16},{4,20},{8,24},{12,28},{16,0},{20,4},{24,8},{28,12},{32,48},... | collective-permute-start | bytes 589832 | tf_op jit(solution)/shard_map/ppermute | solution.py:136
  32.9 8.7 %collective-permute-done.5 = f32[1,128,384]{2,1,0:T(8,128)S(1)} collective-permute-done((f32[1,128,384]{2,1,0:T(8,128)S(1)}, f32[1,128,384]{2,1,0:T(8,128)S(1)}, u32[]{:S(2)}, u32[]{:S(2)}) %collective-permute-start.5) | collective-permute-done | bytes 196640 | tf_op jit(solution)/shard_map/ppermute | solution.py:136
  42.9 6.3 %collective-permute-start.6 = (f32[1,128,384]{2,1,0:T(8,128)S(1)}, f32[1,128,384]{2,1,0:T(8,128)S(1)}, u32[]{:S(2)}, u32[]{:S(2)}) collective-permute-start(f32[1,128,384]{2,1,0:T(8,128)S(1)} %pad_maximum_fusion.2), channel_id=1, source_target_pairs={{0,32},{4,36},{8,40},{12,44},{16,48},{20,52},{24,56},{28,60},{32,0... | collective-permute-start | bytes 589832 | tf_op jit(solution)/shard_map/ppermute | solution.py:136
  49.4 7.4 %collective-permute-done.6 = f32[1,128,384]{2,1,0:T(8,128)S(1)} collective-permute-done((f32[1,128,384]{2,1,0:T(8,128)S(1)}, f32[1,128,384]{2,1,0:T(8,128)S(1)}, u32[]{:S(2)}, u32[]{:S(2)}) %collective-permute-start.6) | collective-permute-done | bytes 196640 | tf_op jit(solution)/shard_map/ppermute | solution.py:136
  58.9 4.8 %collective-permute-done.7 = f32[1,128,384]{2,1,0:T(8,128)S(1)} collective-permute-done((f32[1,128,384]{2,1,0:T(8,128)S(1)}, f32[1,128,384]{2,1,0:T(8,128)S(1)}, u32[]{:S(2)}, u32[]{:S(2)}) %collective-permute-start.7) | collective-permute-done | bytes 196640 | tf_op jit(solution)/shard_map/ppermute | solution.py:136
  64.4 2.4 %collective-permute-start.8 = (f32[1,128,256]{2,1,0:T(8,128)S(1)}, f32[1,128,256]{2,1,0:T(8,128)S(1)}, u32[]{:S(2)}, u32[]{:S(2)}) collective-permute-start(f32[1,128,256]{2,1,0:T(8,128)S(1)} %pad_maximum_fusion.4), channel_id=1, source_target_pairs={{0,128},{4,132},{8,136},{12,140},{16,144},{20,148},{24,152},{28,15... | collective-permute-start | bytes 393224 | tf_op jit(solution)/shard_map/ppermute | solution.py:136
  67.7 3.3 %collective-permute-done.8 = f32[1,128,256]{2,1,0:T(8,128)S(1)} collective-permute-done((f32[1,128,256]{2,1,0:T(8,128)S(1)}, f32[1,128,256]{2,1,0:T(8,128)S(1)}, u32[]{:S(2)}, u32[]{:S(2)}) %collective-permute-start.8) | collective-permute-done | bytes 131104 | tf_op jit(solution)/shard_map/ppermute | solution.py:136
  72.4 1.1 %collective-permute-done.9 = f32[1,128,256]{2,1,0:T(8,128)S(1)} collective-permute-done((f32[1,128,256]{2,1,0:T(8,128)S(1)}, f32[1,128,256]{2,1,0:T(8,128)S(1)}, u32[]{:S(2)}, u32[]{:S(2)}) %collective-permute-start.9) | collective-permute-done | bytes 131104 | tf_op jit(solution)/shard_map/ppermute | solution.py:177
  83.9 0.6 copy.539
  84.6 0.6 copy.537
  85.3 0.6 reshape.303
  85.9 2.8 %collective-permute-done.10 = bf16[128,256]{1,0:T(8,128)(2,1)S(1)} collective-permute-done((bf16[128,256]{1,0:T(8,128)(2,1)S(1)}, bf16[128,256]{1,0:T(8,128)(2,1)S(1)}, u32[]{:S(2)}, u32[]{:S(2)}) %collective-permute-start.10) | collective-permute-done | bytes 65568 | tf_op jit(solution)/shard_map/ppermute | solution.py:269
  89.7 5.6 %collective-permute-done.11 = bf16[2,128,256]{2,1,0:T(8,128)(2,1)S(1)} collective-permute-done((bf16[2,128,256]{2,1,0:T(8,128)(2,1)S(1)}, bf16[2,128,256]{2,1,0:T(8,128)(2,1)S(1)}, u32[]{:S(2)}, u32[]{:S(2)}) %collective-permute-start.11) | collective-permute-done | bytes 131104 | tf_op jit(solution)/shard_map/ppermute | solution.py:270
  95.3 1.9 %convolution_convert_fusion = bf16[128,256]{1,0:T(8,128)(2,1)} fusion(bf16[256,256]{1,0:T(8,128)(2,1)} %collective-permute-done.14, bf16[256,256]{1,0:T(8,128)(2,1)} %collective-permute-done.13, bf16[256,256]{1,0:T(8,128)(2,1)} %collective-permute-done.12, bf16[256,256]{1,0:T(8,128)(2,1)S(1)} %get-tuple-element.11, ...), kind=kOutput, calls=%fused_computation.40 | convolution fusion | flops 70287360 | bytes 851968 | tf_op jit(solution)/shard_map/dot_general | solution.py:276
  (158 shorter events, 28.5 us)
Async XLA Ops:
  0.6 17.4 %collective-permute-start.1 = (bf16[128,256]{1,0:T(8,128)(2,1)}, bf16[128,256]{1,0:T(8,128)(2,1)S(1)}, u32[]{:S(2)}, u32[]{:S(2)}) collective-permute-start(bf16[128,256]{1,0:T(8,128)(2,1)} %param.11), channel_id=1, source_target_pairs={{0,2},{1,3},{2,0},{3,1},{4,6},{5,7},{6,4},{7,5},{8,10},{9,11},{10,... | collective-permute-start | bytes 196616 | tf_op jit(solution)/shard_map/ppermute | solution.py:184
  3.7 14.3 %collective-permute-start = (bf16[128,256]{1,0:T(8,128)(2,1)}, bf16[128,256]{1,0:T(8,128)(2,1)S(1)}, u32[]{:S(2)}, u32[]{:S(2)}) collective-permute-start(bf16[128,256]{1,0:T(8,128)(2,1)} %param.11), channel_id=1, source_target_pairs={{0,1},{1,2},{2,3},{3,0},{4,5},{5,6},{6,7},{7,4},{8,9},{9,10},{10,1... | collective-permute-start | bytes 196616 | tf_op jit(solution)/shard_map/ppermute | solution.py:184
  4.3 13.7 %collective-permute-start.2 = (bf16[128,256]{1,0:T(8,128)(2,1)}, bf16[128,256]{1,0:T(8,128)(2,1)S(1)}, u32[]{:S(2)}, u32[]{:S(2)}) collective-permute-start(bf16[128,256]{1,0:T(8,128)(2,1)} %param.11), channel_id=1, source_target_pairs={{0,3},{1,0},{2,1},{3,2},{4,7},{5,4},{6,5},{7,6},{8,11},{9,8},{10,9... | collective-permute-start | bytes 196616 | tf_op jit(solution)/shard_map/ppermute | solution.py:184
  7.0 0.8 copy-start.3
  7.0 0.7 copy-start.4
  7.8 0.8 copy-start.1
  9.0 0.9 copy-start.2
  15.8 1.0 %copy-start = (bf16[256,1024]{1,0:T(8,128)(2,1)S(1)}, bf16[256,1024]{1,0:T(8,128)(2,1)}, u32[]{:S(2)}) copy-start(bf16[256,1024]{1,0:T(8,128)(2,1)} %param.10) | copy-start | bytes 1572868
  17.7 0.8 copy-start.5
  19.4 1.5 %collective-permute-start.3 = (f32[1,128,384]{2,1,0:T(8,128)S(1)}, f32[1,128,384]{2,1,0:T(8,128)S(1)}, u32[]{:S(2)}, u32[]{:S(2)}) collective-permute-start(f32[1,128,384]{2,1,0:T(8,128)S(1)} %fusion.82), channel_id=1, source_target_pairs={{0,4},{4,0},{8,12},{12,8},{16,20},{20,16},{24,28},{28,24},{32,36},... | collective-permute-start | bytes 589832 | tf_op jit(solution)/shard_map/ppermute | solution.py:116
  21.5 7.2 %collective-permute-start.4 = (f32[1,128,384]{2,1,0:T(8,128)S(1)}, f32[1,128,384]{2,1,0:T(8,128)S(1)}, u32[]{:S(2)}, u32[]{:S(2)}) collective-permute-start(f32[1,128,384]{2,1,0:T(8,128)S(1)} %pad_maximum_fusion), channel_id=1, source_target_pairs={{0,8},{4,12},{8,0},{12,4},{16,24},{20,28},{24,16},{28,20},{32,40},... | collective-permute-start | bytes 589832 | tf_op jit(solution)/shard_map/ppermute | solution.py:136
  23.5 71.8 %collective-permute-start.12 = (bf16[256,256]{1,0:T(8,128)(2,1)}, bf16[256,256]{1,0:T(8,128)(2,1)}, u32[]{:S(2)}, u32[]{:S(2)}) collective-permute-start(bf16[256,256]{1,0:T(8,128)(2,1)} %get-tuple-element.10), channel_id=1, source_target_pairs={{0,1},{1,2},{2,3},{3,0},{4,5},{5,6},{6,7},{7,4},{8,9},{9,10},{10,1... | collective-permute-start | bytes 393224 | tf_op jit(solution)/shard_map/ppermute | solution.py:256
  23.5 71.8 %collective-permute-start.14 = (bf16[256,256]{1,0:T(8,128)(2,1)}, bf16[256,256]{1,0:T(8,128)(2,1)}, u32[]{:S(2)}, u32[]{:S(2)}) collective-permute-start(bf16[256,256]{1,0:T(8,128)(2,1)} %get-tuple-element.15), channel_id=1, source_target_pairs={{0,3},{1,0},{2,1},{3,2},{4,7},{5,4},{6,5},{7,6},{8,11},{9,8},{10,9... | collective-permute-start | bytes 393224 | tf_op jit(solution)/shard_map/ppermute | solution.py:256
  26.8 68.5 %collective-permute-start.13 = (bf16[256,256]{1,0:T(8,128)(2,1)}, bf16[256,256]{1,0:T(8,128)(2,1)}, u32[]{:S(2)}, u32[]{:S(2)}) collective-permute-start(bf16[256,256]{1,0:T(8,128)(2,1)} %get-tuple-element.16), channel_id=1, source_target_pairs={{0,2},{1,3},{2,0},{3,1},{4,6},{5,7},{6,4},{7,5},{8,10},{9,11},{10,... | collective-permute-start | bytes 393224 | tf_op jit(solution)/shard_map/ppermute | solution.py:256
  29.4 12.2 %collective-permute-start.5 = (f32[1,128,384]{2,1,0:T(8,128)S(1)}, f32[1,128,384]{2,1,0:T(8,128)S(1)}, u32[]{:S(2)}, u32[]{:S(2)}) collective-permute-start(f32[1,128,384]{2,1,0:T(8,128)S(1)} %pad_maximum_fusion.1), channel_id=1, source_target_pairs={{0,16},{4,20},{8,24},{12,28},{16,0},{20,4},{24,8},{28,12},{32,48},... | collective-permute-start | bytes 589832 | tf_op jit(solution)/shard_map/ppermute | solution.py:136
  42.9 13.9 %collective-permute-start.6 = (f32[1,128,384]{2,1,0:T(8,128)S(1)}, f32[1,128,384]{2,1,0:T(8,128)S(1)}, u32[]{:S(2)}, u32[]{:S(2)}) collective-permute-start(f32[1,128,384]{2,1,0:T(8,128)S(1)} %pad_maximum_fusion.2), channel_id=1, source_target_pairs={{0,32},{4,36},{8,40},{12,44},{16,48},{20,52},{24,56},{28,60},{32,0... | collective-permute-start | bytes 589832 | tf_op jit(solution)/shard_map/ppermute | solution.py:136
  57.9 5.8 %collective-permute-start.7 = (f32[1,128,384]{2,1,0:T(8,128)S(1)}, f32[1,128,384]{2,1,0:T(8,128)S(1)}, u32[]{:S(2)}, u32[]{:S(2)}) collective-permute-start(f32[1,128,384]{2,1,0:T(8,128)S(1)} %pad_maximum_fusion.3), channel_id=1, source_target_pairs={{0,64},{4,68},{8,72},{12,76},{16,80},{20,84},{24,88},{28,92},{32,9... | collective-permute-start | bytes 589832 | tf_op jit(solution)/shard_map/ppermute | solution.py:136
  64.4 6.6 %collective-permute-start.8 = (f32[1,128,256]{2,1,0:T(8,128)S(1)}, f32[1,128,256]{2,1,0:T(8,128)S(1)}, u32[]{:S(2)}, u32[]{:S(2)}) collective-permute-start(f32[1,128,256]{2,1,0:T(8,128)S(1)} %pad_maximum_fusion.4), channel_id=1, source_target_pairs={{0,128},{4,132},{8,136},{12,140},{16,144},{20,148},{24,152},{28,15... | collective-permute-start | bytes 393224 | tf_op jit(solution)/shard_map/ppermute | solution.py:136
  71.9 1.7 %collective-permute-start.9 = (f32[1,128,256]{2,1,0:T(8,128)S(1)}, f32[1,128,256]{2,1,0:T(8,128)S(1)}, u32[]{:S(2)}, u32[]{:S(2)}) collective-permute-start(f32[1,128,256]{2,1,0:T(8,128)S(1)} %pad_maximum_fusion.9), channel_id=1, source_target_pairs={{0,4},{4,0},{8,12},{12,8},{16,20},{20,16},{24,28},{28,24},{32,36},... | collective-permute-start | bytes 393224 | tf_op jit(solution)/shard_map/ppermute | solution.py:177
  83.2 5.6 %collective-permute-start.10 = (bf16[128,256]{1,0:T(8,128)(2,1)S(1)}, bf16[128,256]{1,0:T(8,128)(2,1)S(1)}, u32[]{:S(2)}, u32[]{:S(2)}) collective-permute-start(bf16[128,256]{1,0:T(8,128)(2,1)S(1)} %bitcast.531), channel_id=1, source_target_pairs={{0,1},{1,2},{2,3},{3,0},{4,5},{5,6},{6,7},{7,4},{8,9},{9,10},{10,1... | collective-permute-start | bytes 196616 | tf_op jit(solution)/shard_map/ppermute | solution.py:269
  88.7 6.6 %collective-permute-start.11 = (bf16[2,128,256]{2,1,0:T(8,128)(2,1)S(1)}, bf16[2,128,256]{2,1,0:T(8,128)(2,1)S(1)}, u32[]{:S(2)}, u32[]{:S(2)}) collective-permute-start(bf16[2,128,256]{2,1,0:T(8,128)(2,1)S(1)} %pad_maximum_fusion.10), channel_id=1, source_target_pairs={{0,2},{1,3},{2,0},{3,1},{4,6},{5,7},{6,4},{7,5},{8,10},{9,11},{10,... | collective-permute-start | bytes 393224 | tf_op jit(solution)/shard_map/ppermute | solution.py:270
where the time goes:
time: 97.9 us; the launch traced here: 97.2 us
  waiting for transfers between devices  37.1 us (38%)
  starting transfers between devices  24.8 us (25%)
  matrix products  24.6 us (25%)
  local copies, waits for them, and re-layouts  7.28 us (7%)
  other arithmetic  1.8 us (2%)
  between operations  1.67 us (2%)
    ppermute x5, waiting for transfers between devices, scan_both(): got = lax.ppermute(sent, axis, pairs)  26.2 us
    ppermute x5, starting transfers between devices, scan_both(): got = lax.ppermute(sent, axis, pairs)  14.6 us
    ppermute x3, starting transfers between devices, head_ring(): lax.ppermute(part, axis, [(i, (i + k) % count) for i in range(count)])  6.35 us
    ppermute x1, waiting for transfers between devices, body(): lax.ppermute(jnp.stack([attended_bf, first]), 'head', [(i, (i + 2) % 4) f...  5.6 us
    unnamed x18, local copies, waits for them, and re-layouts  4.98 us
    dot_general x17, matrix products, mm(): return jnp.einsum('hij,hjk->hik', left, right, precision=highest)  3.76 us
    ppermute x3, starting transfers between devices, body(): lax.ppermute(block, 'head', [(i, (i + k) % head_devices) for i in range(h...  3.24 us
    ppermute x1, waiting for transfers between devices, body(): lax.ppermute(attended_bf, 'head', [(i, (i + 1) % 4) for i in range(4)])  2.79 us
  transfers between devices with their start and end apart: 15, of which 9 were waited for; matrix products, arithmetic and copies ran while one was open for 28% of the time, Pallas kernels for 0%

commit v1 on v0

--- a/solution.py
+++ b/solution.py
@@ -194,8 +194,6 @@
         width = queries.shape[1]
         here = lax.axis_index("head")
 
-        grad_parts = head_ring(out_grad, head_devices, "head")
-
         weight_rows = jnp.concatenate(
             [
                 lax.dynamic_slice_in_dim(
@@ -222,6 +220,8 @@
             write_rate,
         )
         unit_query, unit_key, key_mix, value_mix, causal_scores = factors
+        late_grad, _ = lax.optimization_barrier((out_grad, key_mix))
+        grad_parts = head_ring(late_grad, head_devices, "head")
         identity_heads = jnp.broadcast_to(
             jnp.eye(head_width, dtype=jnp.float32), (head_count, head_width, head_width)
         )
@@ -265,14 +265,7 @@
 
         (final_state, block_outputs), pull_run = jax.vjp(run_from_entry, factors)
         attended_bf = from_blocks(block_outputs).astype(jnp.bfloat16)
-        if head_devices == 4:
-            first = lax.ppermute(attended_bf, "head", [(i, (i + 1) % 4) for i in range(4)])
-            second = lax.ppermute(
-                jnp.stack([attended_bf, first]), "head", [(i, (i + 2) % 4) for i in range(4)]
-            )
-            attended_parts = [attended_bf, first, second[0], second[1]]
-        else:
-            attended_parts = head_ring(attended_bf, head_devices, "head")
+        attended_parts = head_ring(attended_bf, head_devices, "head")
         layer_out = jnp.dot(
             jnp.concatenate(attended_parts, 1), weight_mine, preferred_element_type=jnp.float32
         ).astype(jnp.bfloat16)

time: 97.9 us -> 94.7 us (0.967)
  waiting for transfers between devices: 37.1 us -> 30.6 us
  starting transfers between devices: 24.8 us -> 27.2 us
    ppermute x2 -> x0, waiting for transfers between devices: 8.39 us -> none  [the longest x1 5.6 us: body(): lax.ppermute(jnp.stack([attended_bf, first]), 'head', [(i, (i + 2) % 4) f...]
    ppermute x3 -> x6, waiting for transfers between devices: 0.01 us -> 2.66 us  [head_ring(): lax.ppermute(part, axis, [(i, (i + k) % count) for i in range(count)])]
    ppermute x3 -> x6, starting transfers between devices: 6.35 us -> 8.43 us  [head_ring(): lax.ppermute(part, axis, [(i, (i + k) % count) for i in range(count)])]
    unnamed x18 -> x16, local copies, waits for them, and re-layouts: 4.98 us -> 4.99 us
  transfers between devices with their start and end apart: 15 -> 16, of which waited for: 9 -> 8; matrix products, arithmetic and copies ran while one was open for 28% -> 25% of each run, Pallas kernels for 0% -> 0%
where the time goes in v1:
time: 94.7 us; the launch traced here: 93.9 us
  waiting for transfers between devices  30.6 us (32%)
  starting transfers between devices  27.2 us (29%)
  matrix products  24.6 us (26%)
  local copies, waits for them, and re-layouts  8.09 us (9%)
  other arithmetic  1.79 us (2%)
  between operations  1.64 us (2%)
    ppermute x5, waiting for transfers between devices, scan_both(): got = lax.ppermute(sent, axis, pairs)  25.4 us
    ppermute x5, starting transfers between devices, scan_both(): got = lax.ppermute(sent, axis, pairs)  14.7 us
    ppermute x6, starting transfers between devices, head_ring(): lax.ppermute(part, axis, [(i, (i + k) % count) for i in range(count)])  8.43 us
    unnamed x16, local copies, waits for them, and re-layouts  4.99 us
    ppermute x3, starting transfers between devices, body(): lax.ppermute(block, 'head', [(i, (i + k) % head_devices) for i in range(h...  3.88 us
    dot_general x17, matrix products, mm(): return jnp.einsum('hij,hjk->hik', left, right, precision=highest)  3.78 us
    ppermute x6, waiting for transfers between devices, head_ring(): lax.ppermute(part, axis, [(i, (i + k) % count) for i in range(count)])  2.66 us
    dot_general x7, matrix products, advance_block(): jnp.einsum('chd,che->hde', unit_key, innovation, precision=highest)  2.44 us
  transfers between devices with their start and end apart: 16, of which 8 were waited for; matrix products, arithmetic and copies ran while one was open for 25% of the time, Pallas kernels for 0%

profile of v1, /device:TPU:8, one launch (start us, length us, event | category | flops | bytes accessed | tf_op | source)
XLA Modules:
  0.0 93.9 jit_solution(13075362961907831608)
XLA Ops:
  1.4 0.9 reshape.294
  6.5 2.8 %collective-permute-start.2 = (bf16[128,256]{1,0:T(8,128)(2,1)S(1)}, bf16[128,256]{1,0:T(8,128)(2,1)S(1)}, u32[]{:S(2)}, u32[]{:S(2)}) collective-permute-start(bf16[128,256]{1,0:T(8,128)(2,1)S(1)} %copy-done.4), channel_id=1, source_target_pairs={{0,3},{1,0},{2,1},{3,2},{4,7},{5,4},{6,5},{7,6},{8,11},{9,8},{10,9... | collective-permute-start | bytes 196616 | tf_op jit(solution)/shard_map/ppermute | solution.py:184
  9.2 0.8 collective-permute-start.1
  10.0 0.9 collective-permute-start
  10.9 0.8 copy-done.2
  11.8 0.8 copy-done.1
  16.3 0.9 constant_dynamic-slice_fusion.7
  18.4 1.4 %collective-permute-done.3 = f32[1,128,384]{2,1,0:T(8,128)S(1)} collective-permute-done((f32[1,128,384]{2,1,0:T(8,128)S(1)}, f32[1,128,384]{2,1,0:T(8,128)S(1)}, u32[]{:S(2)}, u32[]{:S(2)}) %collective-permute-start.3) | collective-permute-done | bytes 196640 | tf_op jit(solution)/shard_map/ppermute | solution.py:116
  20.5 2.0 %collective-permute-start.4 = (f32[1,128,384]{2,1,0:T(8,128)S(1)}, f32[1,128,384]{2,1,0:T(8,128)S(1)}, u32[]{:S(2)}, u32[]{:S(2)}) collective-permute-start(f32[1,128,384]{2,1,0:T(8,128)S(1)} %pad_maximum_fusion), channel_id=1, source_target_pairs={{0,8},{4,12},{8,0},{12,4},{16,24},{20,28},{24,16},{28,20},{32,40},... | collective-permute-start | bytes 589832 | tf_op jit(solution)/shard_map/ppermute | solution.py:136
  22.5 1.8 %collective-permute-start.13 = (bf16[256,256]{1,0:T(8,128)(2,1)}, bf16[256,256]{1,0:T(8,128)(2,1)}, u32[]{:S(2)}, u32[]{:S(2)}) collective-permute-start(bf16[256,256]{1,0:T(8,128)(2,1)} %get-tuple-element.12), channel_id=1, source_target_pairs={{0,1},{1,2},{2,3},{3,0},{4,5},{5,6},{6,7},{7,4},{8,9},{9,10},{10,1... | collective-permute-start | bytes 393224 | tf_op jit(solution)/shard_map/ppermute | solution.py:256
  24.3 1.4 %collective-permute-start.15 = (bf16[256,256]{1,0:T(8,128)(2,1)}, bf16[256,256]{1,0:T(8,128)(2,1)}, u32[]{:S(2)}, u32[]{:S(2)}) collective-permute-start(bf16[256,256]{1,0:T(8,128)(2,1)} %get-tuple-element.17), channel_id=1, source_target_pairs={{0,3},{1,0},{2,1},{3,2},{4,7},{5,4},{6,5},{7,6},{8,11},{9,8},{10,9... | collective-permute-start | bytes 393224 | tf_op jit(solution)/shard_map/ppermute | solution.py:256
  26.4 1.3 %collective-permute-done.4 = f32[1,128,384]{2,1,0:T(8,128)S(1)} collective-permute-done((f32[1,128,384]{2,1,0:T(8,128)S(1)}, f32[1,128,384]{2,1,0:T(8,128)S(1)}, u32[]{:S(2)}, u32[]{:S(2)}) %collective-permute-start.4) | collective-permute-done | bytes 196640 | tf_op jit(solution)/shard_map/ppermute | solution.py:136
  28.4 3.3 %collective-permute-start.5 = (f32[1,128,384]{2,1,0:T(8,128)S(1)}, f32[1,128,384]{2,1,0:T(8,128)S(1)}, u32[]{:S(2)}, u32[]{:S(2)}) collective-permute-start(f32[1,128,384]{2,1,0:T(8,128)S(1)} %pad_maximum_fusion.1), channel_id=1, source_target_pairs={{0,16},{4,20},{8,24},{12,28},{16,0},{20,4},{24,8},{28,12},{32,48},... | collective-permute-start | bytes 589832 | tf_op jit(solution)/shard_map/ppermute | solution.py:136
  31.8 8.6 %collective-permute-done.5 = f32[1,128,384]{2,1,0:T(8,128)S(1)} collective-permute-done((f32[1,128,384]{2,1,0:T(8,128)S(1)}, f32[1,128,384]{2,1,0:T(8,128)S(1)}, u32[]{:S(2)}, u32[]{:S(2)}) %collective-permute-start.5) | collective-permute-done | bytes 196640 | tf_op jit(solution)/shard_map/ppermute | solution.py:136
  41.8 6.4 %collective-permute-start.6 = (f32[1,128,384]{2,1,0:T(8,128)S(1)}, f32[1,128,384]{2,1,0:T(8,128)S(1)}, u32[]{:S(2)}, u32[]{:S(2)}) collective-permute-start(f32[1,128,384]{2,1,0:T(8,128)S(1)} %pad_maximum_fusion.2), channel_id=1, source_target_pairs={{0,32},{4,36},{8,40},{12,44},{16,48},{20,52},{24,56},{28,60},{32,0... | collective-permute-start | bytes 589832 | tf_op jit(solution)/shard_map/ppermute | solution.py:136
  48.4 7.4 %collective-permute-done.6 = f32[1,128,384]{2,1,0:T(8,128)S(1)} collective-permute-done((f32[1,128,384]{2,1,0:T(8,128)S(1)}, f32[1,128,384]{2,1,0:T(8,128)S(1)}, u32[]{:S(2)}, u32[]{:S(2)}) %collective-permute-start.6) | collective-permute-done | bytes 196640 | tf_op jit(solution)/shard_map/ppermute | solution.py:136
  57.9 4.8 %collective-permute-done.7 = f32[1,128,384]{2,1,0:T(8,128)S(1)} collective-permute-done((f32[1,128,384]{2,1,0:T(8,128)S(1)}, f32[1,128,384]{2,1,0:T(8,128)S(1)}, u32[]{:S(2)}, u32[]{:S(2)}) %collective-permute-start.7) | collective-permute-done | bytes 196640 | tf_op jit(solution)/shard_map/ppermute | solution.py:136
  63.3 2.4 %collective-permute-start.8 = (f32[1,128,256]{2,1,0:T(8,128)S(1)}, f32[1,128,256]{2,1,0:T(8,128)S(1)}, u32[]{:S(2)}, u32[]{:S(2)}) collective-permute-start(f32[1,128,256]{2,1,0:T(8,128)S(1)} %pad_maximum_fusion.4), channel_id=1, source_target_pairs={{0,128},{4,132},{8,136},{12,140},{16,144},{20,148},{24,152},{28,15... | collective-permute-start | bytes 393224 | tf_op jit(solution)/shard_map/ppermute | solution.py:136
  66.6 3.3 %collective-permute-done.8 = f32[1,128,256]{2,1,0:T(8,128)S(1)} collective-permute-done((f32[1,128,256]{2,1,0:T(8,128)S(1)}, f32[1,128,256]{2,1,0:T(8,128)S(1)}, u32[]{:S(2)}, u32[]{:S(2)}) %collective-permute-start.8) | collective-permute-done | bytes 131104 | tf_op jit(solution)/shard_map/ppermute | solution.py:136
  71.1 1.1 %collective-permute-done.9 = f32[1,128,256]{2,1,0:T(8,128)S(1)} collective-permute-done((f32[1,128,256]{2,1,0:T(8,128)S(1)}, f32[1,128,256]{2,1,0:T(8,128)S(1)}, u32[]{:S(2)}, u32[]{:S(2)}) %collective-permute-start.9) | collective-permute-done | bytes 131104 | tf_op jit(solution)/shard_map/ppermute | solution.py:177
  79.2 2.4 %collective-permute-start.12 = (bf16[128,256]{1,0:T(8,128)(2,1)S(1)}, bf16[128,256]{1,0:T(8,128)(2,1)S(1)}, u32[]{:S(2)}, u32[]{:S(2)}) collective-permute-start(bf16[128,256]{1,0:T(8,128)(2,1)S(1)} %bitcast.526), channel_id=1, source_target_pairs={{0,3},{1,0},{2,1},{3,2},{4,7},{5,4},{6,5},{7,6},{8,11},{9,8},{10,9... | collective-permute-start | bytes 196616 | tf_op jit(solution)/shard_map/ppermute | solution.py:184
  81.6 1.5 %collective-permute-start.11 = (bf16[128,256]{1,0:T(8,128)(2,1)S(1)}, bf16[128,256]{1,0:T(8,128)(2,1)S(1)}, u32[]{:S(2)}, u32[]{:S(2)}) collective-permute-start(bf16[128,256]{1,0:T(8,128)(2,1)S(1)} %bitcast.527), channel_id=1, source_target_pairs={{0,2},{1,3},{2,0},{3,1},{4,6},{5,7},{6,4},{7,5},{8,10},{9,11},{10,... | collective-permute-start | bytes 196616 | tf_op jit(solution)/shard_map/ppermute | solution.py:184
  89.4 2.6 %collective-permute-done.10 = bf16[128,256]{1,0:T(8,128)(2,1)S(1)} collective-permute-done((bf16[128,256]{1,0:T(8,128)(2,1)S(1)}, bf16[128,256]{1,0:T(8,128)(2,1)S(1)}, u32[]{:S(2)}, u32[]{:S(2)}) %collective-permute-start.10) | collective-permute-done | bytes 65568 | tf_op jit(solution)/shard_map/ppermute | solution.py:184
  92.0 1.9 %convolution_convert_fusion = bf16[128,256]{1,0:T(8,128)(2,1)} fusion(bf16[256,256]{1,0:T(8,128)(2,1)} %collective-permute-done.15, bf16[256,256]{1,0:T(8,128)(2,1)} %collective-permute-done.14, bf16[256,256]{1,0:T(8,128)(2,1)} %collective-permute-done.13, bf16[256,256]{1,0:T(8,128)(2,1)S(1)} %get-tuple-element.13, ...), kind=kOutput, calls=%fused_computation.40 | convolution fusion | flops 70287360 | bytes 851968 | tf_op jit(solution)/shard_map/dot_general | solution.py:269
  (155 shorter events, 30.7 us)
Async XLA Ops:
  0.6 0.7 copy-start.3
  5.6 0.8 copy-start.4
  6.5 11.0 %collective-permute-start.2 = (bf16[128,256]{1,0:T(8,128)(2,1)S(1)}, bf16[128,256]{1,0:T(8,128)(2,1)S(1)}, u32[]{:S(2)}, u32[]{:S(2)}) collective-permute-start(bf16[128,256]{1,0:T(8,128)(2,1)S(1)} %copy-done.4), channel_id=1, source_target_pairs={{0,3},{1,0},{2,1},{3,2},{4,7},{5,4},{6,5},{7,6},{8,11},{9,8},{10,9... | collective-permute-start | bytes 196616 | tf_op jit(solution)/shard_map/ppermute | solution.py:184
  9.2 8.3 %collective-permute-start.1 = (bf16[128,256]{1,0:T(8,128)(2,1)S(1)}, bf16[128,256]{1,0:T(8,128)(2,1)S(1)}, u32[]{:S(2)}, u32[]{:S(2)}) collective-permute-start(bf16[128,256]{1,0:T(8,128)(2,1)S(1)} %copy-done.4), channel_id=1, source_target_pairs={{0,2},{1,3},{2,0},{3,1},{4,6},{5,7},{6,4},{7,5},{8,10},{9,11},{10,... | collective-permute-start | bytes 196616 | tf_op jit(solution)/shard_map/ppermute | solution.py:184
  10.0 7.5 %collective-permute-start = (bf16[128,256]{1,0:T(8,128)(2,1)S(1)}, bf16[128,256]{1,0:T(8,128)(2,1)S(1)}, u32[]{:S(2)}, u32[]{:S(2)}) collective-permute-start(bf16[128,256]{1,0:T(8,128)(2,1)S(1)} %copy-done.4), channel_id=1, source_target_pairs={{0,1},{1,2},{2,3},{3,0},{4,5},{5,6},{6,7},{7,4},{8,9},{9,10},{10,1... | collective-permute-start | bytes 196616 | tf_op jit(solution)/shard_map/ppermute | solution.py:184
  10.9 0.8 copy-start.2
  11.7 0.8 copy-start.1
  15.3 1.0 %copy-start = (bf16[256,1024]{1,0:T(8,128)(2,1)S(1)}, bf16[256,1024]{1,0:T(8,128)(2,1)}, u32[]{:S(2)}) copy-start(bf16[256,1024]{1,0:T(8,128)(2,1)} %param.10) | copy-start | bytes 1572868
  18.3 1.5 %collective-permute-start.3 = (f32[1,128,384]{2,1,0:T(8,128)S(1)}, f32[1,128,384]{2,1,0:T(8,128)S(1)}, u32[]{:S(2)}, u32[]{:S(2)}) collective-permute-start(f32[1,128,384]{2,1,0:T(8,128)S(1)} %fusion.84), channel_id=1, source_target_pairs={{0,4},{4,0},{8,12},{12,8},{16,20},{20,16},{24,28},{28,24},{32,36},... | collective-permute-start | bytes 589832 | tf_op jit(solution)/shard_map/ppermute | solution.py:116
  20.5 7.2 %collective-permute-start.4 = (f32[1,128,384]{2,1,0:T(8,128)S(1)}, f32[1,128,384]{2,1,0:T(8,128)S(1)}, u32[]{:S(2)}, u32[]{:S(2)}) collective-permute-start(f32[1,128,384]{2,1,0:T(8,128)S(1)} %pad_maximum_fusion), channel_id=1, source_target_pairs={{0,8},{4,12},{8,0},{12,4},{16,24},{20,28},{24,16},{28,20},{32,40},... | collective-permute-start | bytes 589832 | tf_op jit(solution)/shard_map/ppermute | solution.py:136
  22.5 63.9 %collective-permute-start.13 = (bf16[256,256]{1,0:T(8,128)(2,1)}, bf16[256,256]{1,0:T(8,128)(2,1)}, u32[]{:S(2)}, u32[]{:S(2)}) collective-permute-start(bf16[256,256]{1,0:T(8,128)(2,1)} %get-tuple-element.12), channel_id=1, source_target_pairs={{0,1},{1,2},{2,3},{3,0},{4,5},{5,6},{6,7},{7,4},{8,9},{9,10},{10,1... | collective-permute-start | bytes 393224 | tf_op jit(solution)/shard_map/ppermute | solution.py:256
  24.3 65.0 %collective-permute-start.15 = (bf16[256,256]{1,0:T(8,128)(2,1)}, bf16[256,256]{1,0:T(8,128)(2,1)}, u32[]{:S(2)}, u32[]{:S(2)}) collective-permute-start(bf16[256,256]{1,0:T(8,128)(2,1)} %get-tuple-element.17), channel_id=1, source_target_pairs={{0,3},{1,0},{2,1},{3,2},{4,7},{5,4},{6,5},{7,6},{8,11},{9,8},{10,9... | collective-permute-start | bytes 393224 | tf_op jit(solution)/shard_map/ppermute | solution.py:256
  25.7 63.6 %collective-permute-start.14 = (bf16[256,256]{1,0:T(8,128)(2,1)}, bf16[256,256]{1,0:T(8,128)(2,1)}, u32[]{:S(2)}, u32[]{:S(2)}) collective-permute-start(bf16[256,256]{1,0:T(8,128)(2,1)} %get-tuple-element.18), channel_id=1, source_target_pairs={{0,2},{1,3},{2,0},{3,1},{4,6},{5,7},{6,4},{7,5},{8,10},{9,11},{10,... | collective-permute-start | bytes 393224 | tf_op jit(solution)/shard_map/ppermute | solution.py:256
  28.4 12.1 %collective-permute-start.5 = (f32[1,128,384]{2,1,0:T(8,128)S(1)}, f32[1,128,384]{2,1,0:T(8,128)S(1)}, u32[]{:S(2)}, u32[]{:S(2)}) collective-permute-start(f32[1,128,384]{2,1,0:T(8,128)S(1)} %pad_maximum_fusion.1), channel_id=1, source_target_pairs={{0,16},{4,20},{8,24},{12,28},{16,0},{20,4},{24,8},{28,12},{32,48},... | collective-permute-start | bytes 589832 | tf_op jit(solution)/shard_map/ppermute | solution.py:136
  41.8 14.0 %collective-permute-start.6 = (f32[1,128,384]{2,1,0:T(8,128)S(1)}, f32[1,128,384]{2,1,0:T(8,128)S(1)}, u32[]{:S(2)}, u32[]{:S(2)}) collective-permute-start(f32[1,128,384]{2,1,0:T(8,128)S(1)} %pad_maximum_fusion.2), channel_id=1, source_target_pairs={{0,32},{4,36},{8,40},{12,44},{16,48},{20,52},{24,56},{28,60},{32,0... | collective-permute-start | bytes 589832 | tf_op jit(solution)/shard_map/ppermute | solution.py:136
  56.8 5.8 %collective-permute-start.7 = (f32[1,128,384]{2,1,0:T(8,128)S(1)}, f32[1,128,384]{2,1,0:T(8,128)S(1)}, u32[]{:S(2)}, u32[]{:S(2)}) collective-permute-start(f32[1,128,384]{2,1,0:T(8,128)S(1)} %pad_maximum_fusion.3), channel_id=1, source_target_pairs={{0,64},{4,68},{8,72},{12,76},{16,80},{20,84},{24,88},{28,92},{32,9... | collective-permute-start | bytes 589832 | tf_op jit(solution)/shard_map/ppermute | solution.py:136
  63.3 6.6 %collective-permute-start.8 = (f32[1,128,256]{2,1,0:T(8,128)S(1)}, f32[1,128,256]{2,1,0:T(8,128)S(1)}, u32[]{:S(2)}, u32[]{:S(2)}) collective-permute-start(f32[1,128,256]{2,1,0:T(8,128)S(1)} %pad_maximum_fusion.4), channel_id=1, source_target_pairs={{0,128},{4,132},{8,136},{12,140},{16,144},{20,148},{24,152},{28,15... | collective-permute-start | bytes 393224 | tf_op jit(solution)/shard_map/ppermute | solution.py:136
  70.8 1.4 %collective-permute-start.9 = (f32[1,128,256]{2,1,0:T(8,128)S(1)}, f32[1,128,256]{2,1,0:T(8,128)S(1)}, u32[]{:S(2)}, u32[]{:S(2)}) collective-permute-start(f32[1,128,256]{2,1,0:T(8,128)S(1)} %pad_maximum_fusion.9), channel_id=1, source_target_pairs={{0,4},{4,0},{8,12},{12,8},{16,20},{20,16},{24,28},{28,24},{32,36},... | collective-permute-start | bytes 393224 | tf_op jit(solution)/shard_map/ppermute | solution.py:177
  79.2 10.2 %collective-permute-start.12 = (bf16[128,256]{1,0:T(8,128)(2,1)S(1)}, bf16[128,256]{1,0:T(8,128)(2,1)S(1)}, u32[]{:S(2)}, u32[]{:S(2)}) collective-permute-start(bf16[128,256]{1,0:T(8,128)(2,1)S(1)} %bitcast.526), channel_id=1, source_target_pairs={{0,3},{1,0},{2,1},{3,2},{4,7},{5,4},{6,5},{7,6},{8,11},{9,8},{10,9... | collective-permute-start | bytes 196616 | tf_op jit(solution)/shard_map/ppermute | solution.py:184
  81.6 7.7 %collective-permute-start.11 = (bf16[128,256]{1,0:T(8,128)(2,1)S(1)}, bf16[128,256]{1,0:T(8,128)(2,1)S(1)}, u32[]{:S(2)}, u32[]{:S(2)}) collective-permute-start(bf16[128,256]{1,0:T(8,128)(2,1)S(1)} %bitcast.527), channel_id=1, source_target_pairs={{0,2},{1,3},{2,0},{3,1},{4,6},{5,7},{6,4},{7,5},{8,10},{9,11},{10,... | collective-permute-start | bytes 196616 | tf_op jit(solution)/shard_map/ppermute | solution.py:184
  86.5 5.6 %collective-permute-start.10 = (bf16[128,256]{1,0:T(8,128)(2,1)S(1)}, bf16[128,256]{1,0:T(8,128)(2,1)S(1)}, u32[]{:S(2)}, u32[]{:S(2)}) collective-permute-start(bf16[128,256]{1,0:T(8,128)(2,1)S(1)} %bitcast.528), channel_id=1, source_target_pairs={{0,1},{1,2},{2,3},{3,0},{4,5},{5,6},{6,7},{7,4},{8,9},{9,10},{10,1... | collective-permute-start | bytes 196616 | tf_op jit(solution)/shard_map/ppermute | solution.py:184
